TPU v7x, 256 devices: a whole 4x4x8 slice. The times are simulated.
256 devices in a mesh: win: 8 (over y, core), chan: 32 (over x, z).
Axes of the slice: x: 4, y: 4, z: 8, core: 2. Of those that a mesh axis runs over, the one named last changes fastest.
Arguments:
- traces: float32 [8, 15000, 4096], P('win', None, 'chan'), may hold values from -200 to 200
- pair_blocks: int32 [192, 2], P('chan'), may hold values from -1 to 31, as said below
Outputs:
- stacks: float32 [192, 512, 128], P('chan', 'win')
Inputs may be any that keep to these rules, and one draw needn't show every extreme that they name: `pair_blocks`: owner o holds rows o * 6 to (o + 1) * 6 - 1. Each row is a block pair (i, i + d) with 1 <= d <= 3, or (-1, -1) for an empty slot; every block pair with an offset in that range stands in exactly one row; some owner has all 6 of its slots filled.
All inputs are finite; a program needn't handle non-finite values.
Results may differ from a plain program's by a relative error of at most 0.003.
Values may be sent and summed in bfloat16 or wider, within the bound.
No kernel may reach another device: no remote copies, remote signals or barrier semaphores. Data moves between devices by JAX's collectives and lax.ppermute only.
A program may use at most 64 MiB of HBM per device.

v0:
```python
import math
import jax
import jax.numpy as jnp
from jax import lax
from jax.sharding import PartitionSpec as P

L = 15000
NB = 512
F_LO = 64
HALF = 32
LAGS = 512
two_pi = 2.0 * math.pi


def band_tables():
    width = NB + 2 * HALF
    rows = lax.broadcasted_iota(jnp.int32, (NB, width), 0)
    cols = lax.broadcasted_iota(jnp.int32, (NB, width), 1)
    smoother = jnp.where(
        (cols >= rows) & (cols <= rows + 2 * HALF), 1.0 / (2 * HALF + 1), 0.0
    ).astype(jnp.float32)
    taper = jnp.sin(
        math.pi * (lax.broadcasted_iota(jnp.int32, (NB,), 0).astype(jnp.float32) + 0.5) / NB
    )
    bins = F_LO + lax.broadcasted_iota(jnp.int32, (LAGS, NB), 1)
    lagged = lax.broadcasted_iota(jnp.int32, (LAGS, NB), 0) - LAGS // 2
    angle = (bins * lagged % L).astype(jnp.float32) * (two_pi / L)
    table = jnp.stack([jnp.cos(angle), -jnp.sin(angle)], axis=1).astype(jnp.bfloat16)
    return (smoother, taper, table)


def whiten_local(traces, smoother, taper):
    width = NB + 2 * HALF
    windows, total, channels = traces.shape
    block = math.gcd(total, 3000)

    def add_block(index, acc):
        start = index * block
        piece = lax.dynamic_slice_in_dim(traces, start, block, 1)
        bins = F_LO - HALF + lax.broadcasted_iota(jnp.int32, (width, block), 0)
        times = start + lax.broadcasted_iota(jnp.int32, (width, block), 1)
        angle = (bins * times % total).astype(jnp.float32) * (two_pi / total)
        basis = jnp.concatenate([jnp.cos(angle), -jnp.sin(angle)], axis=0)
        return acc + jnp.einsum(
            "qn,wnc->wqc",
            basis,
            piece,
            precision=lax.Precision.HIGHEST,
            preferred_element_type=jnp.float32,
        )

    spec = lax.fori_loop(
        0, total // block, add_block, jnp.zeros((windows, 2 * width, channels), jnp.float32)
    )
    real = spec[:, :width]
    imag = spec[:, width:]
    power = real * real + imag * imag
    level = jnp.einsum("bm,wmc->wbc", smoother, power, precision=lax.Precision.HIGHEST) + 1e-06
    factor = taper[None, :, None] * lax.rsqrt(level)
    white = jnp.stack(
        [real[:, HALF : HALF + NB] * factor, imag[:, HALF : HALF + NB] * factor], axis=1
    )
    return white.astype(jnp.bfloat16)


def cross_spectra(left, right):
    left_re = left[..., 0, :, :].astype(jnp.float32)
    left_im = left[..., 1, :, :].astype(jnp.float32)
    right_re = right[..., 0, :, :].astype(jnp.float32)
    right_im = right[..., 1, :, :].astype(jnp.float32)
    real = left_re * right_re + left_im * right_im
    imag = left_im * right_re - left_re * right_im
    return jnp.stack([real, imag], axis=-3).astype(jnp.bfloat16)


def correlate(cross, table, factor):
    return jnp.einsum("tqb,swqbk->stk", table, cross, preferred_element_type=jnp.float32) * factor


def body(traces, pair_blocks):
    smoother, taper, table = band_tables()
    white = whiten_local(traces, smoother, taper)
    windows_all = traces.shape[0] * lax.axis_size("win")
    factor = 1.0 / math.sqrt(NB * windows_all)
    filled = (pair_blocks[:, 0] >= 0)[:, None, None]
    every = lax.all_gather(white[None], "chan", axis=0, tiled=True)
    left_index = jnp.maximum(pair_blocks[:, 0], 0)
    right_index = jnp.maximum(pair_blocks[:, 1], 0)
    cross = cross_spectra(jnp.take(every, left_index, axis=0), jnp.take(every, right_index, axis=0))
    local = correlate(cross, table, factor)
    local = jnp.where(filled, local, 0.0)
    return lax.psum_scatter(local, "win", scatter_dimension=1, tiled=True)


def solution(mesh):
    in_specs = (P("win", None, "chan"), P("chan", None))
    out_specs = P("chan", "win", None)
    return jax.shard_map(body, mesh=mesh, in_specs=in_specs, out_specs=out_specs, check_vma=False)
```

profile of v0, /device:TPU:6, one launch (start us, length us, event | category | flops | bytes accessed | tf_op | source)
XLA Modules:
  0.0 422.1 jit_solution(8498667945533063919)
XLA Ops:
  6.5 0.0 all-gather.2.cloned.1.call-start
  6.6 253.2 %while.16 = (s32[]{:T(128)}, f32[1,1152,128]{1,2,0:T(8,128)S(1)}, f32[1,15000,128]{2,1,0:T(8,128)}, s32[]{:T(128)}, s32[]{:T(128)}, /*index=5*/s32[]{:T(128)}, s32[]{:T(128)}) while((s32[]{:T(128)}, f32[1,1152,128]{1,2,0:T(8,128)S(1)}, f32[1,15000,128]{2,1,0:T(8,128)}, s32[]{:T(128)}, s32[]{:T(128)}, /*index=5*/s32[]{:T(128)}, ...), condition=%wide.region_1.2_spmd.clone, body=%wide.region_0.1_spmd.clone.sunk | while | flops 5329450496 | bytes 30724180 | solution.py:52
  6.6 30.7 %fusion.84 = (f32[576,3000]{1,0:T(8,128)}, f32[576,3000]{1,0:T(8,128)}) fusion(s32[3000]{0:T(1024)S(1)} %iota_add_fusion.6, s32[576]{0:T(1024)S(1)} %iota_add_fusion.7), kind=kLoop, calls=%fused_computation.13.clone.1 | loop fusion | flops 17280000 | bytes 13838304 | tf_op jit(solution)/shard_map/while/body/eval_jaxpr/cos | solution.py:43
  37.4 19.8 %fusion.85 = f32[1,1152,128]{1,2,0:T(8,128)S(1)} fusion(f32[576,3000]{1,0:T(8,128)} %get-tuple-element.151, f32[576,3000]{1,0:T(8,128)} %get-tuple-element.152, f32[1,15000,128]{2,1,0:T(8,128)} %get-tuple-element.169, s32[]{:T(128)S(6)} %select_n.131, f32[1,1152,128]{1,2,0:T(8,128)S(1)} %get-tuple-element.161, pred[]{:T(512)S(6)} %compare.3), kind=kOutput, calls=%fused_computation.16.clone.1 | convolution fusion | flops 5312166912 | bytes 16871428 | tf_op jit(solution)/shard_map/while/body/eval_jaxpr/qn,wnc->wqc/dot_general | solution.py:44
  57.2 30.7 %fusion.84 = (f32[576,3000]{1,0:T(8,128)}, f32[576,3000]{1,0:T(8,128)}) fusion(s32[3000]{0:T(1024)S(1)} %iota_add_fusion.6, s32[576]{0:T(1024)S(1)} %iota_add_fusion.7), kind=kLoop, calls=%fused_computation.13.clone.1 | loop fusion | flops 17280000 | bytes 13838304 | tf_op jit(solution)/shard_map/while/body/eval_jaxpr/cos | solution.py:43
  88.0 19.8 %fusion.85 = f32[1,1152,128]{1,2,0:T(8,128)S(1)} fusion(f32[576,3000]{1,0:T(8,128)} %get-tuple-element.151, f32[576,3000]{1,0:T(8,128)} %get-tuple-element.152, f32[1,15000,128]{2,1,0:T(8,128)} %get-tuple-element.169, s32[]{:T(128)S(6)} %select_n.131, f32[1,1152,128]{1,2,0:T(8,128)S(1)} %get-tuple-element.161, pred[]{:T(512)S(6)} %compare.3), kind=kOutput, calls=%fused_computation.16.clone.1 | convolution fusion | flops 5312166912 | bytes 16871428 | tf_op jit(solution)/shard_map/while/body/eval_jaxpr/qn,wnc->wqc/dot_general | solution.py:44
  107.8 30.7 %fusion.84 = (f32[576,3000]{1,0:T(8,128)}, f32[576,3000]{1,0:T(8,128)}) fusion(s32[3000]{0:T(1024)S(1)} %iota_add_fusion.6, s32[576]{0:T(1024)S(1)} %iota_add_fusion.7), kind=kLoop, calls=%fused_computation.13.clone.1 | loop fusion | flops 17280000 | bytes 13838304 | tf_op jit(solution)/shard_map/while/body/eval_jaxpr/cos | solution.py:43
  138.6 19.8 %fusion.85 = f32[1,1152,128]{1,2,0:T(8,128)S(1)} fusion(f32[576,3000]{1,0:T(8,128)} %get-tuple-element.151, f32[576,3000]{1,0:T(8,128)} %get-tuple-element.152, f32[1,15000,128]{2,1,0:T(8,128)} %get-tuple-element.169, s32[]{:T(128)S(6)} %select_n.131, f32[1,1152,128]{1,2,0:T(8,128)S(1)} %get-tuple-element.161, pred[]{:T(512)S(6)} %compare.3), kind=kOutput, calls=%fused_computation.16.clone.1 | convolution fusion | flops 5312166912 | bytes 16871428 | tf_op jit(solution)/shard_map/while/body/eval_jaxpr/qn,wnc->wqc/dot_general | solution.py:44
  158.4 30.7 %fusion.84 = (f32[576,3000]{1,0:T(8,128)}, f32[576,3000]{1,0:T(8,128)}) fusion(s32[3000]{0:T(1024)S(1)} %iota_add_fusion.6, s32[576]{0:T(1024)S(1)} %iota_add_fusion.7), kind=kLoop, calls=%fused_computation.13.clone.1 | loop fusion | flops 17280000 | bytes 13838304 | tf_op jit(solution)/shard_map/while/body/eval_jaxpr/cos | solution.py:43
  189.2 19.8 %fusion.85 = f32[1,1152,128]{1,2,0:T(8,128)S(1)} fusion(f32[576,3000]{1,0:T(8,128)} %get-tuple-element.151, f32[576,3000]{1,0:T(8,128)} %get-tuple-element.152, f32[1,15000,128]{2,1,0:T(8,128)} %get-tuple-element.169, s32[]{:T(128)S(6)} %select_n.131, f32[1,1152,128]{1,2,0:T(8,128)S(1)} %get-tuple-element.161, pred[]{:T(512)S(6)} %compare.3), kind=kOutput, calls=%fused_computation.16.clone.1 | convolution fusion | flops 5312166912 | bytes 16871428 | tf_op jit(solution)/shard_map/while/body/eval_jaxpr/qn,wnc->wqc/dot_general | solution.py:44
  209.0 30.7 %fusion.84 = (f32[576,3000]{1,0:T(8,128)}, f32[576,3000]{1,0:T(8,128)}) fusion(s32[3000]{0:T(1024)S(1)} %iota_add_fusion.6, s32[576]{0:T(1024)S(1)} %iota_add_fusion.7), kind=kLoop, calls=%fused_computation.13.clone.1 | loop fusion | flops 17280000 | bytes 13838304 | tf_op jit(solution)/shard_map/while/body/eval_jaxpr/cos | solution.py:43
  239.8 19.8 %fusion.85 = f32[1,1152,128]{1,2,0:T(8,128)S(1)} fusion(f32[576,3000]{1,0:T(8,128)} %get-tuple-element.151, f32[576,3000]{1,0:T(8,128)} %get-tuple-element.152, f32[1,15000,128]{2,1,0:T(8,128)} %get-tuple-element.169, s32[]{:T(128)S(6)} %select_n.131, f32[1,1152,128]{1,2,0:T(8,128)S(1)} %get-tuple-element.161, pred[]{:T(512)S(6)} %compare.3), kind=kOutput, calls=%fused_computation.16.clone.1 | convolution fusion | flops 5312166912 | bytes 16871428 | tf_op jit(solution)/shard_map/while/body/eval_jaxpr/qn,wnc->wqc/dot_general | solution.py:44
  259.8 0.0 copy-start.2
  259.8 1.4 fusion.69
  261.3 0.8 copy.21
  262.1 0.0 all-gather.2.cloned.1.call-update
  262.1 0.0 reduce-scatter.2.cloned.1.call-start
  262.2 0.0 copy-done.2
  262.3 5.7 %cosine_convert_fusion = (bf16[512,1,512]{2,0,1:T(8,128)(2,1)}, bf16[512,1,512]{2,0,1:T(8,128)(2,1)}) fusion(s32[512]{0:T(512)S(1)} %iota_add_fusion.2, s32[512]{0:T(512)S(1)} %iota_add_fusion.3), kind=kLoop, calls=%fused_computation.57 | loop fusion | flops 3145728 | bytes 1052672 | tf_op jit(solution)/shard_map/convert
  268.0 93.6 %all-gather.2.cloned.1.call-done = bf16[32,1,2,512,128]{4,3,2,1,0:T(8,128)(2,1)} async-done(((bf16[1,1,2,512,128]{4,3,2,1,0:T(8,128)(2,1)}), bf16[32,1,2,512,128]{4,3,2,1,0:T(8,128)(2,1)}) %all-gather.2.cloned.1.call-update) | async-done | bytes 8388624 | tf_op jit(solution)/shard_map/all_gather | solution.py:86
  361.6 4.2 %gather_fusion.1 = bf16[6,2,512,128]{3,2,1,0:T(8,128)(2,1)S(1)} fusion(bf16[32,2,512,128]{3,2,1,0:T(8,128)(2,1)} %bitcast.65, s32[1024]{0:T(1024)S(1)} %pad_clamp_fusion), kind=kCustom, calls=%fused_computation.1.clone | custom fusion | bytes 3145752 | tf_op jit(solution)/shard_map/jit(_take)/gather | solution.py:89
  365.9 0.7 copy.23
  366.6 4.2 %gather_fusion = bf16[6,2,512,128]{3,2,1,0:T(8,128)(2,1)S(1)} fusion(bf16[32,2,512,128]{3,2,1,0:T(8,128)(2,1)} %bitcast.66, s32[1024]{0:T(1024)S(1)} %pad_clamp_fusion.1), kind=kCustom, calls=%fused_computation.clone | custom fusion | bytes 3145752 | tf_op jit(solution)/shard_map/jit(_take)/gather | solution.py:89
  370.8 1.6 copy.22
  372.4 1.7 bitcast_select_fusion
  374.2 0.0 copy-start
  374.2 0.0 copy-start.1
  374.2 0.6 fusion.59
  374.8 0.4 copy-done
  375.2 0.2 copy-done.1
  375.4 1.0 fusion.29
  376.4 1.8 copy.24
  378.2 0.0 reduce-scatter.2.cloned.1.call-update
  378.2 35.3 %reduce-scatter.2.cloned.1.call-done = f32[6,64,128]{2,0,1:T(8,128)} async-done(((f32[6,512,128]{2,0,1:T(8,128)}), f32[6,64,128]{2,0,1:T(8,128)}) %reduce-scatter.2.cloned.1.call-update) | async-done | bytes 196624 | tf_op jit(solution)/shard_map/reduce_scatter | solution.py:92
  413.6 1.7 copy.25
  (19 shorter events, 0.1 us)
Async XLA Ops:
  6.5 355.1 %all-gather.2.cloned.1.call-start = ((), (), s32[]{:S(2)}) async-start(), calls=%async_computation.1 | async-start | bytes 8650752 | tf_op jit(solution)/shard_map/all_gather | solution.py:86
  259.8 2.4 copy-start.2
  262.1 151.4 %reduce-scatter.2.cloned.1.call-start = ((), (), s32[]{:S(2)}) async-start(), calls=%async_computation.2 | async-start | bytes 2359296 | tf_op jit(solution)/shard_map/reduce_scatter | solution.py:92
  374.2 1.0 copy-start
  374.2 1.2 copy-start.1
Sparse Core Ops, SparseCore 0:
  262.2 99.3 all-gather.1
  378.4 35.1 reduce-scatter.1
where the time goes:
time: 422 us
  other arithmetic  162 us (38%)
  waiting for transfers between devices  129 us (31%)
  matrix products  101 us (24%)
  local copies, waits for them, and re-layouts  15.7 us (4%)
  between operations  13.5 us (3%)
    cos x5, other arithmetic, add_block(): basis = jnp.concatenate([jnp.cos(angle), -jnp.sin(angle)], axis=0)  154 us
    dot_general x5, matrix products, add_block(): jnp.einsum('qn,wnc->wqc', basis, piece, precision=lax.Precision.HIGHEST,...  99.1 us
    all_gather x1, waiting for transfers between devices, body(): every = lax.all_gather(white[None], 'chan', axis=0, tiled=True)  93.6 us
    reduce_scatter x1, waiting for transfers between devices, body(): return lax.psum_scatter(local, 'win', scatter_dimension=1, tiled=True)  35.3 us
  transfers between devices with their start and end apart: 2, of which 2 were waited for; matrix products, arithmetic and copies ran while one was open for 1% of the time, Pallas kernels for 0%

commit v1 on v0

--- a/solution.py
+++ b/solution.py
@@ -83,7 +83,9 @@
     windows_all = traces.shape[0] * lax.axis_size("win")
     factor = 1.0 / math.sqrt(NB * windows_all)
     filled = (pair_blocks[:, 0] >= 0)[:, None, None]
-    every = lax.all_gather(white[None], "chan", axis=0, tiled=True)
+    every = jnp.concatenate(
+        lax.all_to_all(jnp.stack([white[None]] * lax.axis_size("chan")), "chan", 0, 0), axis=0
+    )
     left_index = jnp.maximum(pair_blocks[:, 0], 0)
     right_index = jnp.maximum(pair_blocks[:, 1], 0)
     cross = cross_spectra(jnp.take(every, left_index, axis=0), jnp.take(every, right_index, axis=0))

time: 422 us -> 535 us (1.27)
  waiting for transfers between devices: 129 us -> 225 us
  starting transfers between devices: 0.04 us -> 11.8 us
    all_to_all x0 -> x1, waiting for transfers between devices: none -> 186 us  [body(): lax.all_to_all(jnp.stack([white[None]] * lax.axis_size('chan')), 'chan',...]
    all_gather x1 -> x0, waiting for transfers between devices: 93.6 us -> none  [body(): every = lax.all_gather(white[None], 'chan', axis=0, tiled=True)]
    all_to_all x0 -> x1, starting transfers between devices: none -> 11.8 us  [body(): lax.all_to_all(jnp.stack([white[None]] * lax.axis_size('chan')), 'chan',...]
where the time goes in v1:
time: 535 us; the launch traced here: 534 us
  waiting for transfers between devices  225 us (42%)
  other arithmetic  162 us (30%)
  matrix products  102 us (19%)
  local copies, waits for them, and re-layouts  20.2 us (4%)
  between operations  13.5 us (3%)
  starting transfers between devices  11.8 us (2%)
    all_to_all x1, waiting for transfers between devices, body(): lax.all_to_all(jnp.stack([white[None]] * lax.axis_size('chan')), 'chan',...  186 us
    cos x5, other arithmetic, add_block(): basis = jnp.concatenate([jnp.cos(angle), -jnp.sin(angle)], axis=0)  154 us
    dot_general x5, matrix products, add_block(): jnp.einsum('qn,wnc->wqc', basis, piece, precision=lax.Precision.HIGHEST,...  99.1 us
    reduce_scatter x1, waiting for transfers between devices, body(): return lax.psum_scatter(local, 'win', scatter_dimension=1, tiled=True)  38.3 us
    all_to_all x1, starting transfers between devices, body(): lax.all_to_all(jnp.stack([white[None]] * lax.axis_size('chan')), 'chan',...  11.8 us
  transfers between devices with their start and end apart: 2, of which 2 were waited for; matrix products, arithmetic and copies ran while one was open for 1% of the time, Pallas kernels for 0%

profile of v1, /device:TPU:6, one launch (start us, length us, event | category | flops | bytes accessed | tf_op | source)
XLA Modules:
  0.0 534.2 jit_solution(14280153449140302995)
XLA Ops:
  6.6 253.3 %while.16 = (s32[]{:T(128)}, f32[1,1152,128]{1,2,0:T(8,128)S(1)}, f32[1,15000,128]{2,1,0:T(8,128)}, s32[]{:T(128)}, s32[]{:T(128)}, /*index=5*/s32[]{:T(128)}, s32[]{:T(128)}) while((s32[]{:T(128)}, f32[1,1152,128]{1,2,0:T(8,128)S(1)}, f32[1,15000,128]{2,1,0:T(8,128)}, s32[]{:T(128)}, s32[]{:T(128)}, /*index=5*/s32[]{:T(128)}, ...), condition=%wide.region_1.2_spmd.clone, body=%wide.region_0.1_spmd.clone.sunk | while | flops 5329450496 | bytes 30724172 | solution.py:52
  6.6 30.8 %fusion.78 = (f32[576,3000]{1,0:T(8,128)}, f32[576,3000]{1,0:T(8,128)}) fusion(s32[3000]{0:T(1024)S(1)} %iota_add_fusion.6, s32[576]{0:T(1024)S(1)} %iota_add_fusion.7), kind=kLoop, calls=%fused_computation.13.clone.1 | loop fusion | flops 17280000 | bytes 13838304 | tf_op jit(solution)/shard_map/while/body/eval_jaxpr/cos | solution.py:43
  37.4 19.8 %fusion.79 = f32[1,1152,128]{1,2,0:T(8,128)S(1)} fusion(f32[576,3000]{1,0:T(8,128)} %get-tuple-element.151, f32[576,3000]{1,0:T(8,128)} %get-tuple-element.152, f32[1,15000,128]{2,1,0:T(8,128)} %get-tuple-element.169, s32[]{:T(128)S(6)} %select_n.131, f32[1,1152,128]{1,2,0:T(8,128)S(1)} %get-tuple-element.161, pred[]{:T(512)S(6)} %compare.3), kind=kOutput, calls=%fused_computation.16.clone.1 | convolution fusion | flops 5312166912 | bytes 16871428 | tf_op jit(solution)/shard_map/while/body/eval_jaxpr/qn,wnc->wqc/dot_general | solution.py:44
  57.2 30.8 %fusion.78 = (f32[576,3000]{1,0:T(8,128)}, f32[576,3000]{1,0:T(8,128)}) fusion(s32[3000]{0:T(1024)S(1)} %iota_add_fusion.6, s32[576]{0:T(1024)S(1)} %iota_add_fusion.7), kind=kLoop, calls=%fused_computation.13.clone.1 | loop fusion | flops 17280000 | bytes 13838304 | tf_op jit(solution)/shard_map/while/body/eval_jaxpr/cos | solution.py:43
  88.0 19.8 %fusion.79 = f32[1,1152,128]{1,2,0:T(8,128)S(1)} fusion(f32[576,3000]{1,0:T(8,128)} %get-tuple-element.151, f32[576,3000]{1,0:T(8,128)} %get-tuple-element.152, f32[1,15000,128]{2,1,0:T(8,128)} %get-tuple-element.169, s32[]{:T(128)S(6)} %select_n.131, f32[1,1152,128]{1,2,0:T(8,128)S(1)} %get-tuple-element.161, pred[]{:T(512)S(6)} %compare.3), kind=kOutput, calls=%fused_computation.16.clone.1 | convolution fusion | flops 5312166912 | bytes 16871428 | tf_op jit(solution)/shard_map/while/body/eval_jaxpr/qn,wnc->wqc/dot_general | solution.py:44
  107.9 30.8 %fusion.78 = (f32[576,3000]{1,0:T(8,128)}, f32[576,3000]{1,0:T(8,128)}) fusion(s32[3000]{0:T(1024)S(1)} %iota_add_fusion.6, s32[576]{0:T(1024)S(1)} %iota_add_fusion.7), kind=kLoop, calls=%fused_computation.13.clone.1 | loop fusion | flops 17280000 | bytes 13838304 | tf_op jit(solution)/shard_map/while/body/eval_jaxpr/cos | solution.py:43
  138.6 19.8 %fusion.79 = f32[1,1152,128]{1,2,0:T(8,128)S(1)} fusion(f32[576,3000]{1,0:T(8,128)} %get-tuple-element.151, f32[576,3000]{1,0:T(8,128)} %get-tuple-element.152, f32[1,15000,128]{2,1,0:T(8,128)} %get-tuple-element.169, s32[]{:T(128)S(6)} %select_n.131, f32[1,1152,128]{1,2,0:T(8,128)S(1)} %get-tuple-element.161, pred[]{:T(512)S(6)} %compare.3), kind=kOutput, calls=%fused_computation.16.clone.1 | convolution fusion | flops 5312166912 | bytes 16871428 | tf_op jit(solution)/shard_map/while/body/eval_jaxpr/qn,wnc->wqc/dot_general | solution.py:44
  158.5 30.8 %fusion.78 = (f32[576,3000]{1,0:T(8,128)}, f32[576,3000]{1,0:T(8,128)}) fusion(s32[3000]{0:T(1024)S(1)} %iota_add_fusion.6, s32[576]{0:T(1024)S(1)} %iota_add_fusion.7), kind=kLoop, calls=%fused_computation.13.clone.1 | loop fusion | flops 17280000 | bytes 13838304 | tf_op jit(solution)/shard_map/while/body/eval_jaxpr/cos | solution.py:43
  189.2 19.8 %fusion.79 = f32[1,1152,128]{1,2,0:T(8,128)S(1)} fusion(f32[576,3000]{1,0:T(8,128)} %get-tuple-element.151, f32[576,3000]{1,0:T(8,128)} %get-tuple-element.152, f32[1,15000,128]{2,1,0:T(8,128)} %get-tuple-element.169, s32[]{:T(128)S(6)} %select_n.131, f32[1,1152,128]{1,2,0:T(8,128)S(1)} %get-tuple-element.161, pred[]{:T(512)S(6)} %compare.3), kind=kOutput, calls=%fused_computation.16.clone.1 | convolution fusion | flops 5312166912 | bytes 16871428 | tf_op jit(solution)/shard_map/while/body/eval_jaxpr/qn,wnc->wqc/dot_general | solution.py:44
  209.1 30.8 %fusion.78 = (f32[576,3000]{1,0:T(8,128)}, f32[576,3000]{1,0:T(8,128)}) fusion(s32[3000]{0:T(1024)S(1)} %iota_add_fusion.6, s32[576]{0:T(1024)S(1)} %iota_add_fusion.7), kind=kLoop, calls=%fused_computation.13.clone.1 | loop fusion | flops 17280000 | bytes 13838304 | tf_op jit(solution)/shard_map/while/body/eval_jaxpr/cos | solution.py:43
  239.9 19.8 %fusion.79 = f32[1,1152,128]{1,2,0:T(8,128)S(1)} fusion(f32[576,3000]{1,0:T(8,128)} %get-tuple-element.151, f32[576,3000]{1,0:T(8,128)} %get-tuple-element.152, f32[1,15000,128]{2,1,0:T(8,128)} %get-tuple-element.169, s32[]{:T(128)S(6)} %select_n.131, f32[1,1152,128]{1,2,0:T(8,128)S(1)} %get-tuple-element.161, pred[]{:T(512)S(6)} %compare.3), kind=kOutput, calls=%fused_computation.16.clone.1 | convolution fusion | flops 5312166912 | bytes 16871428 | tf_op jit(solution)/shard_map/while/body/eval_jaxpr/qn,wnc->wqc/dot_general | solution.py:44
  259.9 1.4 multiply_convert_fusion.1
  261.3 0.2 copy.11
  261.5 5.3 stack.24
  266.8 0.0 copy-start.2
  266.8 11.8 %all-to-all-start = ((bf16[32,1,1,2,512,128]{5,4,3,2,1,0:T(8,128)(2,1)}), bf16[32,1,1,2,512,128]{5,4,3,2,1,0:T(8,128)(2,1)}, u32[]{:S(2)}, u32[]{:S(2)}) async-start(bf16[32,1,1,2,512,128]{5,4,3,2,1,0:T(8,128)(2,1)} %stack.24), calls=%async_computation | async-start | bytes 16777216 | tf_op jit(solution)/shard_map/all_to_all | solution.py:87
  278.6 0.0 reduce-scatter.2.cloned.1.call-start
  278.6 0.0 copy-done.2
  278.7 5.8 %cosine_convert_fusion = (bf16[512,1,512]{2,0,1:T(8,128)(2,1)}, bf16[512,1,512]{2,0,1:T(8,128)(2,1)}) fusion(s32[512]{0:T(512)S(1)} %iota_add_fusion.2, s32[512]{0:T(512)S(1)} %iota_add_fusion.3), kind=kLoop, calls=%fused_computation.57 | loop fusion | flops 3145728 | bytes 1052672 | tf_op jit(solution)/shard_map/convert
  284.5 186.3 %all-to-all-done = bf16[32,1,1,2,512,128]{5,4,3,2,1,0:T(8,128)(2,1)} async-done(((bf16[32,1,1,2,512,128]{5,4,3,2,1,0:T(8,128)(2,1)}), bf16[32,1,1,2,512,128]{5,4,3,2,1,0:T(8,128)(2,1)}, u32[]{:S(2)}, u32[]{:S(2)}) %all-to-all-start) | async-done | bytes 8388640 | tf_op jit(solution)/shard_map/all_to_all | solution.py:87
  470.8 4.2 gather_fusion
  475.1 0.7 copy.12
  475.8 4.2 gather_fusion.1
  480.0 1.6 copy.13
  481.6 1.7 bitcast_select_fusion
  483.4 0.0 copy-start
  483.4 0.0 copy-start.1
  483.4 0.6 fusion.59
  484.0 0.4 copy-done
  484.4 0.2 copy-done.1
  484.6 1.0 fusion.29
  485.6 1.8 copy.15
  487.4 0.0 reduce-scatter.2.cloned.1.call-update
  487.4 38.3 %reduce-scatter.2.cloned.1.call-done = f32[6,64,128]{2,0,1:T(8,128)} async-done(((f32[6,512,128]{2,0,1:T(8,128)}), f32[6,64,128]{2,0,1:T(8,128)}) %reduce-scatter.2.cloned.1.call-update) | async-done | bytes 196624 | tf_op jit(solution)/shard_map/reduce_scatter | solution.py:94
  525.7 1.7 copy.16
  (19 shorter events, 0.1 us)
Async XLA Ops:
  266.8 11.9 %copy-start.2 = (s32[6,2]{0,1:T(2,128)S(1)}, s32[6,2]{0,1:T(2,128)}, u32[]{:S(2)}) copy-start(s32[6,2]{0,1:T(2,128)} %param.7) | copy-start | bytes 148
  266.8 204.1 %all-to-all-start = ((bf16[32,1,1,2,512,128]{5,4,3,2,1,0:T(8,128)(2,1)}), bf16[32,1,1,2,512,128]{5,4,3,2,1,0:T(8,128)(2,1)}, u32[]{:S(2)}, u32[]{:S(2)}) async-start(bf16[32,1,1,2,512,128]{5,4,3,2,1,0:T(8,128)(2,1)} %stack.24), calls=%async_computation | async-start | bytes 16777216 | tf_op jit(solution)/shard_map/all_to_all | solution.py:87
  278.6 247.1 %reduce-scatter.2.cloned.1.call-start = ((), (), s32[]{:S(2)}) async-start(), calls=%async_computation.2 | async-start | bytes 2359296 | tf_op jit(solution)/shard_map/reduce_scatter | solution.py:94
  483.4 1.0 copy-start
  483.4 1.2 copy-start.1
Sparse Core Ops, SparseCore 0:
  487.6 38.1 reduce-scatter.1
